TPU v7x, 128 devices: a whole 4x4x4 slice. The times are simulated.
128 devices in a mesh: dp: 2 (over x_hi), pipe: 4 (over z), tensor: 16 (over y, x_lo, core).
Axes of the slice: x: 4 (x_hi: 2, x_lo: 2; x = x_hi * 2 + x_lo), y: 4, z: 4, core: 2. Of those that a mesh axis runs over, the one named last changes fastest.
Arguments:
- tokens: bfloat16 [2, 4, 2048, 4096], P('dp', 'pipe', 'tensor'), may hold values from -6 to 6
- norm_gain: float32 [4, 4096], P('pipe'), may hold values from 0.25 to 1.75
- query_weight: bfloat16 [4, 4096, 6144], P('pipe', None, 'tensor'), may hold values from -5.625 to 5.625
- kv_weight: bfloat16 [4, 4096, 2048], P('pipe'), may hold values from -0.09375 to 0.09375
- out_weight: bfloat16 [4, 6144, 4096], P('pipe', 'tensor'), may hold values from -0.75 to 0.75
Outputs:
- next_input: bfloat16 [2, 4, 2048, 4096], P('dp', 'pipe', 'tensor')
- max_logits: float32 [4, 48], P('pipe', 'tensor')
All inputs are finite; a program needn't handle non-finite values.
Results may differ from a plain program's by a relative error of at most 0.018.
The roundings to bfloat16 on the way count: a program that leaves them out, or rounds other values in their place, can miss the bound.
Values may be sent and summed in bfloat16 or wider, within the bound.
No kernel may reach another device: no remote copies, remote signals or barrier semaphores. Data moves between devices by JAX's collectives and lax.ppermute only.
A program may use at most 128 MiB of HBM per device.

v0:
```python
import math

import jax
import jax.numpy as jnp
from jax import lax
from jax.sharding import Mesh
from jax.sharding import PartitionSpec as P


HD = 128
CHIPS = ("ty", "tx")
CORE = "tc"
TENSOR = CHIPS + (CORE,)
BLOCK_SPLIT = (56, 48, 24)
N_BLOCKS = len(BLOCK_SPLIT)


def from_behind(block, axis, distance):
    devices = range(lax.axis_size(axis))
    route = [((i - distance) % len(devices), i) for i in devices]
    return lax.ppermute(block, axis, route)


def scatter_sum(partial):
    n_chips = partial.shape[0]
    chip = lax.axis_index(CHIPS)
    total = lax.dynamic_index_in_dim(partial, chip, 0, keepdims=False).astype(jnp.float32)
    for k in range(1, n_chips):
        send = lax.dynamic_index_in_dim(partial, (chip + k) % n_chips, 0, keepdims=False)
        route = [(i, (i + k) % n_chips) for i in range(n_chips)]
        got = lax.ppermute(send, CHIPS, route)
        total = total + got.astype(jnp.float32)
    return total


def other_core(block):
    return lax.ppermute(block, CORE, [(0, 1), (1, 0)])


def on_device_body(tokens, norm_gain, query_weight, kv_weight, out_weight):
    inputs = tokens[0, 0]
    wide_in = inputs.astype(jnp.float32)
    normed = (
        wide_in
        * lax.rsqrt(jnp.mean(wide_in * wide_in, axis=1, keepdims=True) + 1e-05)
        * norm_gain[0][None, :]
    ).astype(jnp.bfloat16)
    query_local = query_weight[0]
    out_local = out_weight[0]
    heads_dev = query_local.shape[1] // HD
    chip_heads = 2 * heads_dev
    query_cols = chip_heads * HD
    chip = lax.axis_index(CHIPS)
    core = lax.axis_index(CORE)
    kv_local = lax.dynamic_slice_in_dim(kv_weight[0], chip * 2 * HD, 2 * HD, 1)
    query_chip = jnp.concatenate([query_local, other_core(query_local)], 1)
    out_chip = jnp.concatenate([out_local, other_core(out_local)], 0)
    gathered = lax.all_gather(normed, TENSOR, axis=0, tiled=True)
    seq_len = gathered.shape[0]
    local_rows = inputs.shape[0]
    n_chips = seq_len // (2 * local_rows)
    own_rows = lax.dynamic_index_in_dim(
        gathered.reshape(n_chips, 2, local_rows, gathered.shape[1]), core, 1, keepdims=False
    )
    projected = jnp.dot(
        own_rows, jnp.concatenate([query_chip, kv_local], 1), preferred_element_type=jnp.float32
    ).astype(jnp.bfloat16)
    queries = projected[..., :query_cols]
    own_kv = projected[..., query_cols:]
    other_kv = other_core(own_kv)
    keyvals = jnp.where(
        core == 0, jnp.stack([own_kv, other_kv], 1), jnp.stack([other_kv, own_kv], 1)
    ).reshape(seq_len, 2 * HD)
    query_heads = queries.reshape(n_chips, local_rows, chip_heads, HD)
    kv_heads = keyvals.reshape(seq_len, 2, HD)
    key_heads = kv_heads[:, 0]
    value_heads = kv_heads[:, 1]
    score_scale = 1.0 / math.sqrt(HD)
    bounds = [0]
    for size in BLOCK_SPLIT:
        bounds.append(bounds[-1] + size * local_rows // sum(BLOCK_SPLIT))
    col_ids = jnp.arange(seq_len)
    pieces = []
    peaks = []
    for b in range(N_BLOCKS):
        lo, hi = bounds[b], bounds[b + 1]
        sub = hi - lo
        block_rows = n_chips * sub
        query_block = query_heads[:, lo:hi].reshape(block_rows, chip_heads, HD)
        row_ids = (
            (jnp.arange(n_chips)[:, None] * 2 + core) * local_rows
            + lo
            + jnp.arange(sub)[None, :]
        ).reshape(block_rows)
        scores = (
            jnp.einsum("qgd,sd->gqs", query_block, key_heads, preferred_element_type=jnp.float32)
            * score_scale
        )
        allowed = col_ids[None, :] <= row_ids[:, None]
        scores = jnp.where(allowed, scores, -jnp.inf)
        row_max = jnp.max(scores, axis=2, keepdims=True)
        expw = jnp.exp(scores - row_max)
        row_sum = jnp.sum(expw, axis=2, keepdims=True)
        blended = jnp.einsum(
            "gqs,sd->qgd",
            expw.astype(jnp.bfloat16),
            value_heads,
            preferred_element_type=jnp.float32,
        )
        blended = blended / jnp.transpose(row_sum, (1, 0, 2))
        attended = blended.astype(jnp.bfloat16).reshape(block_rows, query_cols)
        peaks.append(jnp.max(row_max[..., 0], axis=1))
        partial = jnp.dot(attended, out_chip, preferred_element_type=jnp.float32).astype(jnp.bfloat16)
        summed = scatter_sum(partial.reshape(n_chips, sub, partial.shape[1]))
        result = (wide_in[lo:hi] + summed).astype(jnp.bfloat16)
        pieces.append(from_behind(result, "pipe", 1))
    chip_peaks = jnp.max(jnp.stack(peaks), axis=0)
    own_peaks = jnp.maximum(chip_peaks[:heads_dev], other_core(chip_peaks[heads_dev:]))
    peak_all = jnp.maximum(own_peaks, from_behind(own_peaks, "dp", 1))
    passed = jnp.concatenate(pieces, 0)
    return (passed[None, None], peak_all[None])


def solution(mesh):
    n_tensor = mesh.shape["tensor"]
    fine = Mesh(
        mesh.devices.reshape(mesh.shape["dp"], mesh.shape["pipe"], n_tensor // 4, 2, 2),
        ("dp", "pipe") + TENSOR,
    )
    placed = (
        P("dp", "pipe", TENSOR, None),
        P("pipe", None),
        P("pipe", None, TENSOR),
        P("pipe", None, None),
        P("pipe", TENSOR, None),
    )
    return jax.shard_map(
        on_device_body,
        mesh=fine,
        in_specs=placed,
        out_specs=(P("dp", "pipe", TENSOR, None), P("pipe", TENSOR)),
        check_vma=False,
    )
```

profile of v0, /device:TPU:18, one launch (start us, length us, event | category | flops | bytes accessed | tf_op | source)
XLA Modules:
  0.0 362.7 jit_solution(3727949577076633802)
XLA Ops:
  7.2 1.5 fusion.28
  8.7 2.5 fusion.30
  12.2 1.0 iota_compare_fusion.2
  13.3 0.6 iota_compare_fusion.1
  13.8 1.7 dynamic-slice_bitcast_fusion
  15.6 1.8 collective-permute-done
  17.4 87.3 %all-gather.2.cloned.1.call-done = bf16[2048,4096]{1,0:T(8,128)(2,1)} async-done(((bf16[128,4096]{1,0:T(8,128)(2,1)}), bf16[2048,4096]{1,0:T(8,128)(2,1)}) %all-gather.2.cloned.1.call-update) | async-done | bytes 16777232 | tf_op jit(solution)/shard_map/all_gather | solution.py:58
  104.7 14.1 %fusion.31 = bf16[8,128,1024]{2,1,0:T(8,128)(2,1)S(1)} fusion(bf16[4096,256]{1,0:T(8,128)(2,1)S(1)} %dynamic-slice_bitcast_fusion, bf16[4096,384]{1,0:T(8,128)(2,1)} %collective-permute-done, bf16[4096,384]{1,0:T(8,128)(2,1)} %bitcast.244, bf16[8,2,128,4096]{3,2,1,0:T(8,128)(2,1)} %bitcast.242, s32[]{:T(128)S(6)} %select_n.134), kind=kOutput, calls=%fused_computation.44 | convolution fusion | flops 8616148992 | bytes 18874372 | tf_op jit(solution)/shard_map/dot_general | solution.py:65
  118.8 1.3 copy-done.9
  120.1 1.1 slice_bitcast_fusion.3
  121.7 0.6 iota_compare_fusion
  122.3 2.6 slice.64
  125.0 1.9 copy.17
  126.9 1.7 slice.69
  128.6 1.7 slice.67
  130.3 1.4 copy.18
  131.7 2.3 copy.23
  134.0 2.4 copy.20
  136.4 1.7 maximum_select_fusion
  138.1 1.0 copy.14
  139.1 1.3 select_n.137
  140.5 1.5 fusion.96
  142.0 3.0 fusion.24
  145.0 3.4 fusion.23
  148.5 2.3 fusion.49
  150.8 3.4 convolution_convert_fusion.2
  154.2 1.2 dynamic-slice_bitcast_fusion.21
  155.3 1.6 collective-permute-start.19
  157.6 3.0 fusion.7
  160.6 6.3 %fusion.6 = (f32[6]{0:T(128)S(1)}, f32[6,384]{1,0:T(8,128)S(1)}) fusion(f32[2048,384,6]{1,0,2:T(8,128)S(1)} %get-tuple-element.36, pred[384,2048]{0,1:T(8,128)(4,1)S(1)} %iota_compare_fusion.1, f32[6,384]{1,0:T(8,128)S(1)} %get-tuple-element.35), kind=kLoop, calls=%fused_computation.10 | loop fusion | flops 23590650 | bytes 19679256 | tf_op jit(solution)/shard_map/reduce_max | solution.py:112
  166.8 6.7 %divide_convert_fusion.1 = bf16[384,6,128]{0,2,1:T(8,128)(2,1)} fusion(f32[2048,384,6]{1,0,2:T(8,128)S(1)} %get-tuple-element.36, f32[6,384]{1,0:T(8,128)S(1)} %get-tuple-element.35, pred[384,2048]{0,1:T(8,128)(4,1)S(1)} %iota_compare_fusion.1, f32[384,6]{0,1:T(8,128)S(1)} %bitcast.240, bf16[2048,1,128]{2,1,0:T(2,128)(2,1)} %copy-done.11), kind=kOutput, calls=%fused_computation.50 | convolution fusion | flops 1227423744 | bytes 20793344 | tf_op jit(solution)/shard_map/gqs,sd->qgd/dot_general | solution.py:104
  173.6 5.8 %convolution_convert_fusion.1 = bf16[384,4096]{1,0:T(8,128)(2,1)S(1)} fusion(bf16[384,768]{0,1:T(8,128)(2,1)} %bitcast.249, bf16[384,4096]{1,0:T(8,128)(2,1)} %collective-permute-done.2, bf16[384,4096]{1,0:T(8,128)(2,1)} %bitcast.246), kind=kOutput, calls=%fused_computation.32 | convolution fusion | flops 2430074880 | bytes 10027008 | tf_op jit(solution)/shard_map/dot_general | solution.py:113
  179.4 1.6 dynamic-slice_bitcast_fusion.14
  181.0 2.5 collective-permute-start.11
  183.9 4.3 %fusion.5 = (f32[6,448]{1,0:T(8,128)S(1)}, f32[2048,448,6]{0,1,2:T(8,128)S(1)}) fusion(pred[448,2048]{1,0:T(8,128)(4,1)S(1)} %iota_compare_fusion, bf16[448,6,128]{2,0,1:T(8,128)(2,1)S(1)} %bitcast.228, bf16[2048,1,128]{2,1,0:T(2,128)(2,1)S(1)} %copy-done.3), kind=kOutput, calls=%fused_computation.9 | convolution fusion | flops 1425798528 | bytes 24160768 | tf_op jit(solution)/shard_map/qgd,sd->gqs/dot_general | solution.py:96
  188.3 8.2 %fusion.4 = (f32[6]{0:T(128)S(1)}, f32[6,448]{1,0:T(8,128)S(1)}) fusion(f32[2048,448,6]{0,1,2:T(8,128)S(1)} %get-tuple-element.38, pred[448,2048]{1,0:T(8,128)(4,1)S(1)} %iota_compare_fusion, f32[6,448]{1,0:T(8,128)S(1)} %get-tuple-element.37), kind=kLoop, calls=%fused_computation.8 | loop fusion | flops 27522426 | bytes 22959128 | tf_op jit(solution)/shard_map/reduce_max | solution.py:112
  196.6 9.9 %divide_convert_fusion = bf16[448,6,128]{2,0,1:T(8,128)(2,1)S(1)} fusion(f32[2048,448,6]{0,1,2:T(8,128)} %copy-done, f32[6,448]{1,0:T(8,128)S(1)} %get-tuple-element.37, pred[448,2048]{1,0:T(8,128)(4,1)S(1)} %iota_compare_fusion, f32[448,6]{0,1:T(8,128)S(1)} %bitcast.239, bf16[2048,1,128]{2,1,0:T(2,128)(2,1)S(1)} %copy-done.12), kind=kOutput, calls=%fused_computation.48 | convolution fusion | flops 1431994368 | bytes 24171520 | tf_op jit(solution)/shard_map/gqs,sd->qgd/dot_general | solution.py:104
  206.9 6.0 %convolution_convert_fusion = bf16[448,4096]{1,0:T(8,128)(2,1)S(1)} fusion(bf16[448,768]{0,1:T(8,128)(2,1)S(1)} %bitcast.237, bf16[384,4096]{1,0:T(8,128)(2,1)} %collective-permute-done.2, bf16[384,4096]{1,0:T(8,128)(2,1)} %bitcast.247), kind=kOutput, calls=%fused_computation.31 | convolution fusion | flops 2832990208 | bytes 10649600 | tf_op jit(solution)/shard_map/dot_general | solution.py:113
  213.0 0.6 collective-permute-start.16
  213.6 4.7 %collective-permute-start.15 = (bf16[48,4096]{1,0:T(8,128)(2,1)S(1)}, bf16[48,4096]{1,0:T(8,128)(2,1)S(1)}, u32[]{:S(2)}, u32[]{:S(2)}) collective-permute-start(bf16[48,4096]{1,0:T(8,128)(2,1)S(1)} %copy-done.16), channel_id=1, source_target_pairs={{0,10},{2,12},{4,14},{6,0},{8,2},{10,4},{12,6},{14,8},{1,11},{3,13... | collective-permute-start | bytes 1179656 | tf_op jit(solution)/shard_map/ppermute | solution.py:31
  218.3 1.7 dynamic-slice_bitcast_fusion.7
  220.0 2.0 collective-permute-start.9
  222.3 11.1 %collective-permute-done.16 = bf16[48,4096]{1,0:T(8,128)(2,1)S(1)} collective-permute-done((bf16[48,4096]{1,0:T(8,128)(2,1)S(1)}, bf16[48,4096]{1,0:T(8,128)(2,1)S(1)}, u32[]{:S(2)}, u32[]{:S(2)}) %collective-permute-start.16) | collective-permute-done | bytes 393248 | tf_op jit(solution)/shard_map/ppermute | solution.py:31
  233.5 4.8 %collective-permute-start.13 = (bf16[48,4096]{1,0:T(8,128)(2,1)}, bf16[48,4096]{1,0:T(8,128)(2,1)}, u32[]{:S(2)}, u32[]{:S(2)}) collective-permute-start(bf16[48,4096]{1,0:T(8,128)(2,1)} %get-tuple-element.20), channel_id=1, source_target_pairs={{0,6},{2,8},{4,10},{6,12},{8,14},{10,0},{12,2},{14,4},{1,7},{3,9},... | collective-permute-start | bytes 1179656 | tf_op jit(solution)/shard_map/ppermute | solution.py:31
  238.3 16.2 %collective-permute-start.12 = (bf16[48,4096]{1,0:T(8,128)(2,1)S(1)}, bf16[48,4096]{1,0:T(8,128)(2,1)}, u32[]{:S(2)}, u32[]{:S(2)}) collective-permute-start(bf16[48,4096]{1,0:T(8,128)(2,1)S(1)} %copy-done.13), channel_id=1, source_target_pairs={{0,4},{2,6},{4,8},{6,10},{8,12},{10,14},{12,0},{14,2},{1,5},{3,7},... | collective-permute-start | bytes 1179656 | tf_op jit(solution)/shard_map/ppermute | solution.py:31
  254.8 1.4 collective-permute-done.13
  256.2 9.9 %collective-permute-start.7 = (bf16[56,4096]{1,0:T(8,128)(2,1)}, bf16[56,4096]{1,0:T(8,128)(2,1)S(1)}, u32[]{:S(2)}, u32[]{:S(2)}) collective-permute-start(bf16[56,4096]{1,0:T(8,128)(2,1)} %get-tuple-element.11), channel_id=1, source_target_pairs={{0,10},{2,12},{4,14},{6,0},{8,2},{10,4},{12,6},{14,8},{1,11},{3,13... | collective-permute-start | bytes 1376264 | tf_op jit(solution)/shard_map/ppermute | solution.py:31
  266.0 14.9 %collective-permute-done.12 = bf16[48,4096]{1,0:T(8,128)(2,1)} collective-permute-done((bf16[48,4096]{1,0:T(8,128)(2,1)S(1)}, bf16[48,4096]{1,0:T(8,128)(2,1)}, u32[]{:S(2)}, u32[]{:S(2)}) %collective-permute-start.12) | collective-permute-done | bytes 393248 | tf_op jit(solution)/shard_map/ppermute | solution.py:31
  280.9 2.9 collective-permute-start.6
  283.9 2.3 fusion.65
  286.2 2.1 collective-permute-start.24
  288.3 2.9 collective-permute-start.23
  291.1 23.2 %collective-permute-done.6 = bf16[56,4096]{1,0:T(8,128)(2,1)S(1)} collective-permute-done((bf16[56,4096]{1,0:T(8,128)(2,1)}, bf16[56,4096]{1,0:T(8,128)(2,1)S(1)}, u32[]{:S(2)}, u32[]{:S(2)}) %collective-permute-start.6) | collective-permute-done | bytes 458784 | tf_op jit(solution)/shard_map/ppermute | solution.py:31
  314.3 2.0 collective-permute-start.22
  316.3 5.9 %collective-permute-done.4 = bf16[56,4096]{1,0:T(8,128)(2,1)S(1)} collective-permute-done((bf16[56,4096]{1,0:T(8,128)(2,1)}, bf16[56,4096]{1,0:T(8,128)(2,1)S(1)}, u32[]{:S(2)}, u32[]{:S(2)}) %collective-permute-start.4) | collective-permute-done | bytes 458784 | tf_op jit(solution)/shard_map/ppermute | solution.py:31
  322.3 2.4 collective-permute-start.20
  324.7 1.9 fusion.53
  326.5 2.5 collective-permute-start.28
  329.0 1.6 collective-permute-start.18
  330.6 1.6 collective-permute-start.10
  332.3 1.3 fusion.73
  333.7 1.6 collective-permute-start.26
  335.8 18.8 %collective-permute-done.26 = bf16[24,4096]{1,0:T(8,128)(2,1)S(1)} collective-permute-done((bf16[24,4096]{1,0:T(8,128)(2,1)S(1)}, bf16[24,4096]{1,0:T(8,128)(2,1)S(1)}, u32[]{:S(2)}, u32[]{:S(2)}) %collective-permute-start.26) | collective-permute-done | bytes 196640 | tf_op jit(solution)/shard_map/ppermute | solution.py:21
  354.6 1.0 maximum_bitcast_fusion.4
  (88 shorter events, 4.4 us)
Async XLA Ops:
  7.2 97.5 %all-gather.2.cloned.1.call-start = ((), (), s32[]{:S(2)}) async-start(), calls=%async_computation | async-start | bytes 17825792 | tf_op jit(solution)/shard_map/all_gather | solution.py:58
  11.3 6.1 %collective-permute-start = (bf16[4096,384]{1,0:T(8,128)(2,1)}, bf16[4096,384]{1,0:T(8,128)(2,1)}, u32[]{:S(2)}, u32[]{:S(2)}) collective-permute-start(bf16[4096,384]{1,0:T(8,128)(2,1)} %bitcast.243), channel_id=1, source_target_pairs={{0,1},{1,0},{2,3},{3,2},{4,5},{5,4},{6,7},{7,6},{8,9},{9,8},{10,11... | collective-permute-start | bytes 9437192 | tf_op jit(solution)/shard_map/ppermute | solution.py:37
  11.4 139.4 %collective-permute-start.2 = (bf16[384,4096]{1,0:T(8,128)(2,1)}, bf16[384,4096]{1,0:T(8,128)(2,1)}, u32[]{:S(2)}, u32[]{:S(2)}) collective-permute-start(bf16[384,4096]{1,0:T(8,128)(2,1)} %bitcast.245), channel_id=1, source_target_pairs={{0,1},{1,0},{2,3},{3,2},{4,5},{5,4},{6,7},{7,6},{8,9},{9,8},{10,11... | collective-permute-start | bytes 9437192 | tf_op jit(solution)/shard_map/ppermute | solution.py:37
  118.8 1.4 copy-start.9
  121.2 15.2 %collective-permute-start.1 = (bf16[8,128,256]{2,1,0:T(8,128)(2,1)}, bf16[8,128,256]{2,1,0:T(8,128)(2,1)}, u32[]{:S(2)}, u32[]{:S(2)}) collective-permute-start(bf16[8,128,256]{2,1,0:T(8,128)(2,1)} %get-tuple-element.23), channel_id=1, source_target_pairs={{0,1},{1,0},{2,3},{3,2},{4,5},{5,4},{6,7},{7,6},{8,9},{9,8},{10,11... | collective-permute-start | bytes 1572872 | tf_op jit(solution)/shard_map/ppermute | solution.py:37
  131.7 10.3 %copy-start.4 = (pred[192,2048]{1,0:T(8,128)(4,1)S(1)}, pred[192,2048]{1,0:T(8,128)(4,1)}, u32[]{:S(2)}) copy-start(pred[192,2048]{1,0:T(8,128)(4,1)} %iota_compare_fusion.2) | copy-start | bytes 1179652
  142.0 6.5 %copy-start.11 = (bf16[2048,1,128]{2,1,0:T(2,128)(2,1)}, bf16[2048,1,128]{2,1,0:T(2,128)(2,1)S(1)}, u32[]{:S(2)}) copy-start(bf16[2048,1,128]{2,1,0:T(2,128)(2,1)S(1)} %get-tuple-element.31) | copy-start | bytes 1572868
  142.0 15.6 %copy-start.2 = (bf16[2048,1,128]{2,1,0:T(2,128)(2,1)}, bf16[2048,1,128]{2,1,0:T(2,128)(2,1)S(1)}, u32[]{:S(2)}) copy-start(bf16[2048,1,128]{2,1,0:T(2,128)(2,1)S(1)} %get-tuple-element.32) | copy-start | bytes 1572868
  148.5 2.3 copy-start.18
  150.8 6.8 %copy-start.7 = (bf16[8,48,6,128]{3,1,0,2:T(8,128)(2,1)S(1)}, bf16[8,48,6,128]{3,1,0,2:T(8,128)(2,1)}, u32[]{:S(2)}) copy-start(bf16[8,48,6,128]{3,1,0,2:T(8,128)(2,1)} %copy.20) | copy-start | bytes 1769476
  154.2 3.4 copy-start.10
  155.3 58.3 %collective-permute-start.19 = (bf16[24,4096]{1,0:T(8,128)(2,1)}, bf16[24,4096]{1,0:T(8,128)(2,1)}, u32[]{:S(2)}, u32[]{:S(2)}) collective-permute-start(bf16[24,4096]{1,0:T(8,128)(2,1)} %get-tuple-element.24), channel_id=1, source_target_pairs={{0,2},{2,4},{4,6},{6,8},{8,10},{10,12},{12,14},{14,0},{1,3},{3,5},... | collective-permute-start | bytes 589832 | tf_op jit(solution)/shard_map/ppermute | solution.py:31
  157.0 63.0 %collective-permute-start.25 = (bf16[24,4096]{1,0:T(8,128)(2,1)}, bf16[24,4096]{1,0:T(8,128)(2,1)}, u32[]{:S(2)}, u32[]{:S(2)}) collective-permute-start(bf16[24,4096]{1,0:T(8,128)(2,1)} %get-tuple-element.25), channel_id=1, source_target_pairs={{0,14},{2,0},{4,2},{6,4},{8,6},{10,8},{12,10},{14,12},{1,15},{3,1}... | collective-permute-start | bytes 589832 | tf_op jit(solution)/shard_map/ppermute | solution.py:31
  173.6 10.4 %copy-start.3 = (bf16[2048,1,128]{2,1,0:T(2,128)(2,1)S(1)}, bf16[2048,1,128]{2,1,0:T(2,128)(2,1)}, u32[]{:S(2)}) copy-start(bf16[2048,1,128]{2,1,0:T(2,128)(2,1)} %copy-done.2) | copy-start | bytes 1572868
  173.6 10.4 %copy-start.5 = (bf16[8,56,6,128]{3,1,0,2:T(8,128)(2,1)S(1)}, bf16[8,56,6,128]{3,1,0,2:T(8,128)(2,1)}, u32[]{:S(2)}) copy-start(bf16[8,56,6,128]{3,1,0,2:T(8,128)(2,1)} %copy.18) | copy-start | bytes 2064388
  179.4 4.6 %copy-start.8 = (bf16[384,4096]{1,0:T(8,128)(2,1)}, bf16[384,4096]{1,0:T(8,128)(2,1)S(1)}, u32[]{:S(2)}) copy-start(bf16[384,4096]{1,0:T(8,128)(2,1)S(1)} %convolution_convert_fusion.1) | copy-start | bytes 9437188
  181.0 39.0 %collective-permute-start.11 = (bf16[48,4096]{1,0:T(8,128)(2,1)}, bf16[48,4096]{1,0:T(8,128)(2,1)}, u32[]{:S(2)}, u32[]{:S(2)}) collective-permute-start(bf16[48,4096]{1,0:T(8,128)(2,1)} %get-tuple-element.15), channel_id=1, source_target_pairs={{0,2},{2,4},{4,6},{6,8},{8,10},{10,12},{12,14},{14,0},{1,3},{3,5},... | collective-permute-start | bytes 1179656 | tf_op jit(solution)/shard_map/ppermute | solution.py:31
  183.5 38.5 %collective-permute-start.17 = (bf16[48,4096]{1,0:T(8,128)(2,1)}, bf16[48,4096]{1,0:T(8,128)(2,1)}, u32[]{:S(2)}, u32[]{:S(2)}) collective-permute-start(bf16[48,4096]{1,0:T(8,128)(2,1)} %get-tuple-element.16), channel_id=1, source_target_pairs={{0,14},{2,0},{4,2},{6,4},{8,6},{10,8},{12,10},{14,12},{1,15},{3,1}... | collective-permute-start | bytes 1179656 | tf_op jit(solution)/shard_map/ppermute | solution.py:31
  188.3 8.3 %copy-start = (f32[2048,448,6]{0,1,2:T(8,128)}, f32[2048,448,6]{0,1,2:T(8,128)S(1)}, u32[]{:S(2)}) copy-start(f32[2048,448,6]{0,1,2:T(8,128)S(1)} %get-tuple-element.38) | copy-start | bytes 66060292
  188.3 8.3 %copy-start.12 = (bf16[2048,1,128]{2,1,0:T(2,128)(2,1)S(1)}, bf16[2048,1,128]{2,1,0:T(2,128)(2,1)}, u32[]{:S(2)}) copy-start(bf16[2048,1,128]{2,1,0:T(2,128)(2,1)} %copy-done.11) | copy-start | bytes 1572868
  206.6 6.4 %collective-permute-start.27 = (f32[3]{0:T(128)S(1)}, f32[3]{0:T(128)S(1)}, u32[]{:S(2)}, u32[]{:S(2)}) collective-permute-start(f32[3]{0:T(128)S(1)} %slice.59), channel_id=1, source_target_pairs={{0,1},{1,0},{2,3},{3,2},{4,5},{5,4},{6,7},{7,6},{8,9},{9,8},{10,11... | collective-permute-start | bytes 44 | tf_op jit(solution)/shard_map/ppermute | solution.py:37
  206.9 6.1 %copy-start.17 = (bf16[48,4096]{1,0:T(8,128)(2,1)S(1)}, bf16[48,4096]{1,0:T(8,128)(2,1)}, u32[]{:S(2)}) copy-start(bf16[48,4096]{1,0:T(8,128)(2,1)} %get-tuple-element.17) | copy-start | bytes 1179652
  206.9 6.7 %copy-start.16 = (bf16[48,4096]{1,0:T(8,128)(2,1)S(1)}, bf16[48,4096]{1,0:T(8,128)(2,1)}, u32[]{:S(2)}) copy-start(bf16[48,4096]{1,0:T(8,128)(2,1)} %get-tuple-element.18) | copy-start | bytes 1179652
  206.9 31.4 %copy-start.13 = (bf16[48,4096]{1,0:T(8,128)(2,1)S(1)}, bf16[48,4096]{1,0:T(8,128)(2,1)}, u32[]{:S(2)}) copy-start(bf16[48,4096]{1,0:T(8,128)(2,1)} %get-tuple-element.21) | copy-start | bytes 1179652
  206.9 47.6 %copy-start.1 = (bf16[1,1,128,4096]{3,2,1,0:T(8,128)(2,1)S(1)}, bf16[1,1,128,4096]{3,2,1,0:T(8,128)(2,1)}, u32[]{:S(2)}) copy-start(bf16[1,1,128,4096]{3,2,1,0:T(8,128)(2,1)} %param.5) | copy-start | bytes 3145732
  213.0 5.3 %copy-start.6 = (bf16[448,4096]{1,0:T(8,128)(2,1)}, bf16[448,4096]{1,0:T(8,128)(2,1)S(1)}, u32[]{:S(2)}) copy-start(bf16[448,4096]{1,0:T(8,128)(2,1)S(1)} %convolution_convert_fusion) | copy-start | bytes 11010052
  213.0 20.5 %collective-permute-start.16 = (bf16[48,4096]{1,0:T(8,128)(2,1)S(1)}, bf16[48,4096]{1,0:T(8,128)(2,1)S(1)}, u32[]{:S(2)}, u32[]{:S(2)}) collective-permute-start(bf16[48,4096]{1,0:T(8,128)(2,1)S(1)} %copy-done.17), channel_id=1, source_target_pairs={{0,12},{2,14},{4,0},{6,2},{8,4},{10,6},{12,8},{14,10},{1,13},{3,15... | collective-permute-start | bytes 1179656 | tf_op jit(solution)/shard_map/ppermute | solution.py:31
  213.6 24.7 %collective-permute-start.15 = (bf16[48,4096]{1,0:T(8,128)(2,1)S(1)}, bf16[48,4096]{1,0:T(8,128)(2,1)S(1)}, u32[]{:S(2)}, u32[]{:S(2)}) collective-permute-start(bf16[48,4096]{1,0:T(8,128)(2,1)S(1)} %copy-done.16), channel_id=1, source_target_pairs={{0,10},{2,12},{4,14},{6,0},{8,2},{10,4},{12,6},{14,8},{1,11},{3,13... | collective-permute-start | bytes 1179656 | tf_op jit(solution)/shard_map/ppermute | solution.py:31
  220.0 63.8 %collective-permute-start.3 = (bf16[56,4096]{1,0:T(8,128)(2,1)}, bf16[56,4096]{1,0:T(8,128)(2,1)}, u32[]{:S(2)}, u32[]{:S(2)}) collective-permute-start(bf16[56,4096]{1,0:T(8,128)(2,1)} %get-tuple-element.8), channel_id=1, source_target_pairs={{0,2},{2,4},{4,6},{6,8},{8,10},{10,12},{12,14},{14,0},{1,3},{3,5},... | collective-permute-start | bytes 1376264 | tf_op jit(solution)/shard_map/ppermute | solution.py:31
  220.0 63.8 %collective-permute-start.9 = (bf16[56,4096]{1,0:T(8,128)(2,1)}, bf16[56,4096]{1,0:T(8,128)(2,1)}, u32[]{:S(2)}, u32[]{:S(2)}) collective-permute-start(bf16[56,4096]{1,0:T(8,128)(2,1)} %get-tuple-element.9), channel_id=1, source_target_pairs={{0,14},{2,0},{4,2},{6,4},{8,6},{10,8},{12,10},{14,12},{1,15},{3,1}... | collective-permute-start | bytes 1376264 | tf_op jit(solution)/shard_map/ppermute | solution.py:31
  222.0 32.7 %collective-permute-start.14 = (bf16[48,4096]{1,0:T(8,128)(2,1)}, bf16[48,4096]{1,0:T(8,128)(2,1)}, u32[]{:S(2)}, u32[]{:S(2)}) collective-permute-start(bf16[48,4096]{1,0:T(8,128)(2,1)} %get-tuple-element.19), channel_id=1, source_target_pairs={{0,8},{2,10},{4,12},{6,14},{8,0},{10,2},{12,4},{14,6},{1,9},{3,11}... | collective-permute-start | bytes 1179656 | tf_op jit(solution)/shard_map/ppermute | solution.py:31
  233.5 21.0 %copy-start.14 = (bf16[48,4096]{1,0:T(8,128)(2,1)}, bf16[48,4096]{1,0:T(8,128)(2,1)S(1)}, u32[]{:S(2)}) copy-start(bf16[48,4096]{1,0:T(8,128)(2,1)S(1)} %collective-permute-done.16) | copy-start | bytes 1179652
  233.5 22.7 %collective-permute-start.13 = (bf16[48,4096]{1,0:T(8,128)(2,1)}, bf16[48,4096]{1,0:T(8,128)(2,1)}, u32[]{:S(2)}, u32[]{:S(2)}) collective-permute-start(bf16[48,4096]{1,0:T(8,128)(2,1)} %get-tuple-element.20), channel_id=1, source_target_pairs={{0,6},{2,8},{4,10},{6,12},{8,14},{10,0},{12,2},{14,4},{1,7},{3,9},... | collective-permute-start | bytes 1179656 | tf_op jit(solution)/shard_map/ppermute | solution.py:31
  238.3 16.2 %copy-start.15 = (bf16[48,4096]{1,0:T(8,128)(2,1)}, bf16[48,4096]{1,0:T(8,128)(2,1)S(1)}, u32[]{:S(2)}) copy-start(bf16[48,4096]{1,0:T(8,128)(2,1)S(1)} %collective-permute-done.15) | copy-start | bytes 1179652
  238.3 42.6 %collective-permute-start.12 = (bf16[48,4096]{1,0:T(8,128)(2,1)S(1)}, bf16[48,4096]{1,0:T(8,128)(2,1)}, u32[]{:S(2)}, u32[]{:S(2)}) collective-permute-start(bf16[48,4096]{1,0:T(8,128)(2,1)S(1)} %copy-done.13), channel_id=1, source_target_pairs={{0,4},{2,6},{4,8},{6,10},{8,12},{10,14},{12,0},{14,2},{1,5},{3,7},... | collective-permute-start | bytes 1179656 | tf_op jit(solution)/shard_map/ppermute | solution.py:31
  254.7 31.5 %collective-permute-start.8 = (bf16[56,4096]{1,0:T(8,128)(2,1)}, bf16[56,4096]{1,0:T(8,128)(2,1)S(1)}, u32[]{:S(2)}, u32[]{:S(2)}) collective-permute-start(bf16[56,4096]{1,0:T(8,128)(2,1)} %get-tuple-element.10), channel_id=1, source_target_pairs={{0,12},{2,14},{4,0},{6,2},{8,4},{10,6},{12,8},{14,10},{1,13},{3,15... | collective-permute-start | bytes 1376264 | tf_op jit(solution)/shard_map/ppermute | solution.py:31
  256.2 32.1 %collective-permute-start.7 = (bf16[56,4096]{1,0:T(8,128)(2,1)}, bf16[56,4096]{1,0:T(8,128)(2,1)S(1)}, u32[]{:S(2)}, u32[]{:S(2)}) collective-permute-start(bf16[56,4096]{1,0:T(8,128)(2,1)} %get-tuple-element.11), channel_id=1, source_target_pairs={{0,10},{2,12},{4,14},{6,0},{8,2},{10,4},{12,6},{14,8},{1,11},{3,13... | collective-permute-start | bytes 1376264 | tf_op jit(solution)/shard_map/ppermute | solution.py:31
  280.9 33.4 %collective-permute-start.6 = (bf16[56,4096]{1,0:T(8,128)(2,1)}, bf16[56,4096]{1,0:T(8,128)(2,1)S(1)}, u32[]{:S(2)}, u32[]{:S(2)}) collective-permute-start(bf16[56,4096]{1,0:T(8,128)(2,1)} %get-tuple-element.12), channel_id=1, source_target_pairs={{0,8},{2,10},{4,12},{6,14},{8,0},{10,2},{12,4},{14,6},{1,9},{3,11}... | collective-permute-start | bytes 1376264 | tf_op jit(solution)/shard_map/ppermute | solution.py:31
  283.8 32.5 %collective-permute-start.5 = (bf16[56,4096]{1,0:T(8,128)(2,1)}, bf16[56,4096]{1,0:T(8,128)(2,1)S(1)}, u32[]{:S(2)}, u32[]{:S(2)}) collective-permute-start(bf16[56,4096]{1,0:T(8,128)(2,1)} %get-tuple-element.13), channel_id=1, source_target_pairs={{0,6},{2,8},{4,10},{6,12},{8,14},{10,0},{12,2},{14,4},{1,7},{3,9},... | collective-permute-start | bytes 1376264 | tf_op jit(solution)/shard_map/ppermute | solution.py:31
  283.8 38.5 %collective-permute-start.4 = (bf16[56,4096]{1,0:T(8,128)(2,1)}, bf16[56,4096]{1,0:T(8,128)(2,1)S(1)}, u32[]{:S(2)}, u32[]{:S(2)}) collective-permute-start(bf16[56,4096]{1,0:T(8,128)(2,1)} %get-tuple-element.14), channel_id=1, source_target_pairs={{0,4},{2,6},{4,8},{6,10},{8,12},{10,14},{12,0},{14,2},{1,5},{3,7},... | collective-permute-start | bytes 1376264 | tf_op jit(solution)/shard_map/ppermute | solution.py:31
  286.2 40.3 %collective-permute-start.24 = (bf16[24,4096]{1,0:T(8,128)(2,1)}, bf16[24,4096]{1,0:T(8,128)(2,1)S(1)}, u32[]{:S(2)}, u32[]{:S(2)}) collective-permute-start(bf16[24,4096]{1,0:T(8,128)(2,1)} %get-tuple-element.26), channel_id=1, source_target_pairs={{0,12},{2,14},{4,0},{6,2},{8,4},{10,6},{12,8},{14,10},{1,13},{3,15... | collective-permute-start | bytes 589832 | tf_op jit(solution)/shard_map/ppermute | solution.py:31
  288.3 40.7 %collective-permute-start.23 = (bf16[24,4096]{1,0:T(8,128)(2,1)}, bf16[24,4096]{1,0:T(8,128)(2,1)S(1)}, u32[]{:S(2)}, u32[]{:S(2)}) collective-permute-start(bf16[24,4096]{1,0:T(8,128)(2,1)} %get-tuple-element.27), channel_id=1, source_target_pairs={{0,10},{2,12},{4,14},{6,0},{8,2},{10,4},{12,6},{14,8},{1,11},{3,13... | collective-permute-start | bytes 589832 | tf_op jit(solution)/shard_map/ppermute | solution.py:31
  314.3 16.2 %collective-permute-start.22 = (bf16[24,4096]{1,0:T(8,128)(2,1)}, bf16[24,4096]{1,0:T(8,128)(2,1)S(1)}, u32[]{:S(2)}, u32[]{:S(2)}) collective-permute-start(bf16[24,4096]{1,0:T(8,128)(2,1)} %get-tuple-element.28), channel_id=1, source_target_pairs={{0,8},{2,10},{4,12},{6,14},{8,0},{10,2},{12,4},{14,6},{1,9},{3,11}... | collective-permute-start | bytes 589832 | tf_op jit(solution)/shard_map/ppermute | solution.py:31
  316.3 15.8 %collective-permute-start.21 = (bf16[24,4096]{1,0:T(8,128)(2,1)}, bf16[24,4096]{1,0:T(8,128)(2,1)S(1)}, u32[]{:S(2)}, u32[]{:S(2)}) collective-permute-start(bf16[24,4096]{1,0:T(8,128)(2,1)} %get-tuple-element.29), channel_id=1, source_target_pairs={{0,6},{2,8},{4,10},{6,12},{8,14},{10,0},{12,2},{14,4},{1,7},{3,9},... | collective-permute-start | bytes 589832 | tf_op jit(solution)/shard_map/ppermute | solution.py:31
  322.3 10.0 %collective-permute-start.20 = (bf16[24,4096]{1,0:T(8,128)(2,1)}, bf16[24,4096]{1,0:T(8,128)(2,1)S(1)}, u32[]{:S(2)}, u32[]{:S(2)}) collective-permute-start(bf16[24,4096]{1,0:T(8,128)(2,1)} %get-tuple-element.30), channel_id=1, source_target_pairs={{0,4},{2,6},{4,8},{6,10},{8,12},{10,14},{12,0},{14,2},{1,5},{3,7},... | collective-permute-start | bytes 589832 | tf_op jit(solution)/shard_map/ppermute | solution.py:31
  326.5 8.7 %collective-permute-start.28 = (f32[3]{0:T(128)S(1)}, f32[3]{0:T(128)S(1)}, u32[]{:S(2)}, u32[]{:S(2)}) collective-permute-start(f32[3]{0:T(128)S(1)} %slice_maximum_fusion), channel_id=1, source_target_pairs={{64,0},{0,64},{65,1},{1,65},{66,2},{2,66},{67,3},{3,67},{68,4},{4,... | collective-permute-start | bytes 44 | tf_op jit(solution)/shard_map/ppermute | solution.py:21
  329.0 25.6 %collective-permute-start.18 = (bf16[48,4096]{1,0:T(8,128)(2,1)S(1)}, bf16[48,4096]{1,0:T(8,128)(2,1)S(1)}, u32[]{:S(2)}, u32[]{:S(2)}) collective-permute-start(bf16[48,4096]{1,0:T(8,128)(2,1)S(1)} %fusion.65), channel_id=1, source_target_pairs={{48,0},{0,16},{16,32},{32,48},{49,1},{1,17},{17,33},{33,49},{50,2}... | collective-permute-start | bytes 1179656 | tf_op jit(solution)/shard_map/ppermute | solution.py:21
  330.6 24.1 %collective-permute-start.10 = (bf16[56,4096]{1,0:T(8,128)(2,1)S(1)}, bf16[56,4096]{1,0:T(8,128)(2,1)S(1)}, u32[]{:S(2)}, u32[]{:S(2)}) collective-permute-start(bf16[56,4096]{1,0:T(8,128)(2,1)S(1)} %fusion.53), channel_id=1, source_target_pairs={{48,0},{0,16},{16,32},{32,48},{49,1},{1,17},{17,33},{33,49},{50,2}... | collective-permute-start | bytes 1376264 | tf_op jit(solution)/shard_map/ppermute | solution.py:21
  333.7 21.0 %collective-permute-start.26 = (bf16[24,4096]{1,0:T(8,128)(2,1)S(1)}, bf16[24,4096]{1,0:T(8,128)(2,1)S(1)}, u32[]{:S(2)}, u32[]{:S(2)}) collective-permute-start(bf16[24,4096]{1,0:T(8,128)(2,1)S(1)} %fusion.73), channel_id=1, source_target_pairs={{48,0},{0,16},{16,32},{32,48},{49,1},{1,17},{17,33},{33,49},{50,2}... | collective-permute-start | bytes 589832 | tf_op jit(solution)/shard_map/ppermute | solution.py:21
Sparse Core Ops, SparseCore 0:
  11.4 93.2 all-gather.1
where the time goes:
time: 369 us; the launch traced here: 363 us
  waiting for transfers between devices  165 us (45%)
  starting transfers between devices  64.2 us (17%)
  matrix products  58.5 us (16%)
  other arithmetic  33.4 us (9%)
  local copies, waits for them, and re-layouts  27.2 us (7%)
  between operations  14.7 us (4%)
    all_gather x1, waiting for transfers between devices, on_device_body(): gathered = lax.all_gather(normed, TENSOR, axis=0, tiled=True)  87.3 us
    ppermute x21, waiting for transfers between devices, scatter_sum(): got = lax.ppermute(send, CHIPS, route)  56.7 us
    ppermute x21, starting transfers between devices, scatter_sum(): got = lax.ppermute(send, CHIPS, route)  56 us
    dot_general x3, matrix products, on_device_body(): jnp.einsum('gqs,sd->qgd', expw.astype(jnp.bfloat16), value_heads, preferr...  18.9 us
    ppermute x4, waiting for transfers between devices, from_behind(): return lax.ppermute(block, axis, route)  18.8 us
    reduce_max x3, other arithmetic, on_device_body(): peaks.append(jnp.max(row_max[..., 0], axis=1))  18 us
    dot_general x3, matrix products, on_device_body(): jnp.dot(attended, out_chip, preferred_element_type=jnp.float32)  15.2 us
    dot_general x1, matrix products, on_device_body(): jnp.dot(own_rows, jnp.concatenate([query_chip, kv_local], 1), preferred_e...  14.1 us
  transfers between devices with their start and end apart: 30, of which 9 were waited for; matrix products, arithmetic and copies ran while one was open for 30% of the time, Pallas kernels for 0%

commit v1 on v0

--- a/solution.py
+++ b/solution.py
@@ -11,7 +11,7 @@
 CHIPS = ("ty", "tx")
 CORE = "tc"
 TENSOR = CHIPS + (CORE,)
-BLOCK_SPLIT = (56, 48, 24)
+BLOCK_SPLIT = (64, 40, 24)
 N_BLOCKS = len(BLOCK_SPLIT)
 
 
@@ -62,15 +62,8 @@
     own_rows = lax.dynamic_index_in_dim(
         gathered.reshape(n_chips, 2, local_rows, gathered.shape[1]), core, 1, keepdims=False
     )
-    projected = jnp.dot(
-        own_rows, jnp.concatenate([query_chip, kv_local], 1), preferred_element_type=jnp.float32
-    ).astype(jnp.bfloat16)
-    queries = projected[..., :query_cols]
-    own_kv = projected[..., query_cols:]
-    other_kv = other_core(own_kv)
-    keyvals = jnp.where(
-        core == 0, jnp.stack([own_kv, other_kv], 1), jnp.stack([other_kv, own_kv], 1)
-    ).reshape(seq_len, 2 * HD)
+    queries = jnp.dot(own_rows, query_chip, preferred_element_type=jnp.float32).astype(jnp.bfloat16)
+    keyvals = jnp.dot(gathered, kv_local, preferred_element_type=jnp.float32).astype(jnp.bfloat16)
     query_heads = queries.reshape(n_chips, local_rows, chip_heads, HD)
     kv_heads = keyvals.reshape(seq_len, 2, HD)
     key_heads = kv_heads[:, 0]

time: 369 us -> 363 us (0.984)
  the two profiles are of different devices: /device:TPU:18 before, /device:TPU:2 now
where the time goes in v1:
time: 363 us; the launch traced here: 360 us
  waiting for transfers between devices  183 us (50%)
  matrix products  67.1 us (18%)
  starting transfers between devices  45.3 us (12%)
  other arithmetic  32.5 us (9%)
  local copies, waits for them, and re-layouts  16.7 us (5%)
  between operations  14.8 us (4%)
    all_gather x1, waiting for transfers between devices, on_device_body(): gathered = lax.all_gather(normed, TENSOR, axis=0, tiled=True)  87.8 us
    ppermute x21, waiting for transfers between devices, scatter_sum(): got = lax.ppermute(send, CHIPS, route)  75 us
    ppermute x21, starting transfers between devices, scatter_sum(): got = lax.ppermute(send, CHIPS, route)  37.5 us
    reduce_max x3, other arithmetic, on_device_body(): peaks.append(jnp.max(row_max[..., 0], axis=1))  18.4 us
    dot_general x3, matrix products, on_device_body(): jnp.einsum('gqs,sd->qgd', expw.astype(jnp.bfloat16), value_heads, preferr...  18.4 us
    ppermute x4, waiting for transfers between devices, from_behind(): return lax.ppermute(block, axis, route)  18.2 us
    dot_general x3, matrix products, on_device_body(): jnp.dot(attended, out_chip, preferred_element_type=jnp.float32)  13.9 us
    dot_general x1, matrix products, on_device_body(): jnp.dot(own_rows, query_chip, preferred_element_type=jnp.float32)  12.3 us
  transfers between devices with their start and end apart: 29, of which 8 were waited for; matrix products, arithmetic and copies ran while one was open for 29% of the time, Pallas kernels for 0%

profile of v1, /device:TPU:2, one launch (start us, length us, event | category | flops | bytes accessed | tf_op | source)
XLA Modules:
  0.0 359.9 jit_solution(396937795666514548)
XLA Ops:
  7.2 1.5 fusion.27
  8.7 2.5 fusion.29
  11.4 0.5 collective-permute-start.1
  12.4 0.3 iota_compare_fusion.2
  12.7 0.4 iota_compare_fusion.1
  13.1 1.8 iota_compare_fusion
  14.9 2.5 collective-permute-done
  17.4 87.8 %all-gather.2.cloned.1.call-done = bf16[2048,4096]{1,0:T(8,128)(2,1)} async-done(((bf16[128,4096]{1,0:T(8,128)(2,1)}), bf16[2048,4096]{1,0:T(8,128)(2,1)}) %all-gather.2.cloned.1.call-update) | async-done | bytes 16777232 | tf_op jit(solution)/shard_map/all_gather | solution.py:58
  105.2 12.3 %fusion.31 = bf16[8,128,768]{2,1,0:T(8,128)(2,1)} fusion(bf16[4096,384]{1,0:T(8,128)(2,1)} %collective-permute-done, bf16[4096,384]{1,0:T(8,128)(2,1)} %bitcast.250, bf16[8,2,128,4096]{3,2,1,0:T(8,128)(2,1)} %bitcast.248, s32[]{:T(128)S(6)} %select_n.122), kind=kOutput, calls=%fused_computation.44 | convolution fusion | flops 6455820288 | bytes 16252932 | tf_op jit(solution)/shard_map/dot_general | solution.py:65
  117.5 1.9 copy.17
  119.4 1.7 slice.59
  121.1 1.7 slice.57
  122.8 1.4 copy.18
  124.2 1.7 copy.23
  125.9 1.7 copy.20
  127.6 10.9 %convolution_convert_fusion.3 = bf16[2048,256]{0,1:T(8,128)(2,1)S(1)} fusion(bf16[2048,4096]{1,0:T(8,128)(2,1)} %all-gather.2.cloned.1.call-done, bf16[1,4096,2048]{2,1,0:T(8,128)(2,1)} %param.8, s32[]{:T(128)S(6)} %select_n.121), kind=kOutput, calls=%fused_computation.36 | convolution fusion | flops 4295491584 | bytes 19922948 | tf_op jit(solution)/shard_map/dot_general | solution.py:66
  138.5 1.8 fusion.22
  140.4 3.6 %fusion.21 = (f32[6]{0:T(128)S(1)}, f32[6,192]{1,0:T(8,128)S(1)}) fusion(f32[2048,192,6]{0,1,2:T(8,128)S(1)} %get-tuple-element.30, pred[192,2048]{1,0:T(8,128)(4,1)S(1)} %iota_compare_fusion.2, f32[6,192]{1,0:T(8,128)S(1)} %get-tuple-element.29), kind=kLoop, calls=%fused_computation.27 | loop fusion | flops 11795322 | bytes 9839640 | tf_op jit(solution)/shard_map/reduce_max | solution.py:105
  144.0 2.4 fusion.57
  146.5 3.3 convolution_convert_fusion.2
  149.8 1.2 dynamic-slice_bitcast_fusion.20
  151.0 1.6 collective-permute-start.18
  152.6 0.4 collective-permute-start.24
  153.0 3.0 fusion.10
  156.0 5.9 %fusion.9 = (f32[6]{0:T(128)S(1)}, f32[6,320]{1,0:T(8,128)S(1)}) fusion(f32[2048,320,6]{0,1,2:T(8,128)S(1)} %get-tuple-element.32, pred[320,2048]{1,0:T(8,128)(4,1)S(1)} %iota_compare_fusion.1, f32[6,320]{1,0:T(8,128)S(1)} %get-tuple-element.31), kind=kLoop, calls=%fused_computation.12 | loop fusion | flops 19658874 | bytes 16399384 | tf_op jit(solution)/shard_map/reduce_max | solution.py:105
  161.9 4.1 %divide_convert_fusion = bf16[320,6,128]{2,0,1:T(8,128)(2,1)S(1)} fusion(f32[2048,320,6]{0,1,2:T(8,128)S(1)} %get-tuple-element.32, f32[6,320]{1,0:T(8,128)S(1)} %get-tuple-element.31, pred[320,2048]{1,0:T(8,128)(4,1)S(1)} %iota_compare_fusion.1, f32[320,6]{0,1:T(8,128)S(1)} %bitcast.246, bf16[2048,2,128]{0,2,1:T(8,128)(2,1)S(1)} %bitcast.237), kind=kOutput, calls=%fused_computation.64 | convolution fusion | flops 1022853120 | bytes 17424384 | tf_op jit(solution)/shard_map/gqs,sd->qgd/dot_general | solution.py:97
  166.0 0.3 copy.22
  166.3 5.1 %convolution_convert_fusion.1 = bf16[320,4096]{1,0:T(8,128)(2,1)S(1)} fusion(bf16[320,768]{0,1:T(8,128)(2,1)S(1)} %bitcast.243, bf16[384,4096]{1,0:T(8,128)(2,1)} %collective-permute-done.1, bf16[384,4096]{1,0:T(8,128)(2,1)} %bitcast.252), kind=kOutput, calls=%fused_computation.30 | convolution fusion | flops 2027159552 | bytes 9404416 | tf_op jit(solution)/shard_map/dot_general | solution.py:106
  171.4 1.4 dynamic-slice_bitcast_fusion.13
  172.8 2.5 collective-permute-start.10
  175.6 6.8 %fusion.3 = (f32[6,512]{1,0:T(8,128)S(1)}, f32[2048,512,6]{1,0,2:T(8,128)S(1)}) fusion(pred[512,2048]{0,1:T(8,128)(4,1)} %iota_compare_fusion, bf16[512,6,128]{2,0,1:T(8,128)(2,1)} %bitcast.228, bf16[2048,2,128]{0,2,1:T(8,128)(2,1)} %bitcast.238), kind=kOutput, calls=%fused_computation.5 | convolution fusion | flops 1629484032 | bytes 27537408 | tf_op jit(solution)/shard_map/qgd,sd->gqs/dot_general | solution.py:89
  182.5 8.9 %fusion.2 = (f32[6]{0:T(128)S(1)}, f32[6,512]{1,0:T(8,128)S(1)}) fusion(f32[2048,512,6]{1,0,2:T(8,128)S(1)} %get-tuple-element.34, pred[512,2048]{0,1:T(8,128)(4,1)} %iota_compare_fusion, f32[6,512]{1,0:T(8,128)S(1)} %get-tuple-element.33), kind=kLoop, calls=%fused_computation.4 | loop fusion | flops 31454202 | bytes 26239000 | tf_op jit(solution)/shard_map/reduce_max | solution.py:105
  191.4 11.9 %fusion.34 = bf16[512,6,128]{0,2,1:T(8,128)(2,1)S(1)} fusion(f32[2048,512,6]{1,0,2:T(8,128)} %copy-done, f32[6,512]{1,0:T(8,128)S(1)} %get-tuple-element.33, pred[512,2048]{0,1:T(8,128)(4,1)} %iota_compare_fusion, f32[512,6]{0,1:T(8,128)S(1)} %bitcast.245, bf16[2048,2,128]{0,2,1:T(8,128)(2,1)} %bitcast.239), kind=kOutput, calls=%fused_computation.46 | convolution fusion | flops 1636564992 | bytes 27549696 | tf_op jit(solution)/shard_map/gqs,sd->qgd/dot_general | solution.py:97
  203.5 5.5 %convolution_convert_fusion = bf16[512,4096]{1,0:T(8,128)(2,1)S(1)} fusion(bf16[512,768]{0,1:T(8,128)(2,1)S(1)} %bitcast.255, bf16[384,4096]{1,0:T(8,128)(2,1)} %collective-permute-done.1, bf16[384,4096]{1,0:T(8,128)(2,1)S(1)} %bitcast.254), kind=kOutput, calls=%fused_computation.29 | convolution fusion | flops 3235905536 | bytes 11272192 | tf_op jit(solution)/shard_map/dot_general | solution.py:106
  209.0 2.8 collective-permute-start.15
  211.8 1.7 collective-permute-start.14
  213.5 1.9 dynamic-slice_bitcast_fusion.6
  215.4 1.2 collective-permute-start.2
  216.6 1.1 collective-permute-start.8
  217.6 3.2 collective-permute-start.13
  220.9 23.8 %collective-permute-done.15 = bf16[40,4096]{1,0:T(8,128)(2,1)S(1)} collective-permute-done((bf16[40,4096]{1,0:T(8,128)(2,1)S(1)}, bf16[40,4096]{1,0:T(8,128)(2,1)S(1)}, u32[]{:S(2)}, u32[]{:S(2)}) %collective-permute-start.15) | collective-permute-done | bytes 327712 | tf_op jit(solution)/shard_map/ppermute | solution.py:31
  244.7 0.7 copy-done.8
  245.4 0.7 copy-done.9
  246.4 3.7 %collective-permute-start.7 = (bf16[64,4096]{1,0:T(8,128)(2,1)}, bf16[64,4096]{1,0:T(8,128)(2,1)S(1)}, u32[]{:S(2)}, u32[]{:S(2)}) collective-permute-start(bf16[64,4096]{1,0:T(8,128)(2,1)} %get-tuple-element.10), channel_id=1, source_target_pairs={{0,12},{2,14},{4,0},{6,2},{8,4},{10,6},{12,8},{14,10},{1,13},{3,15... | collective-permute-start | bytes 1572872 | tf_op jit(solution)/shard_map/ppermute | solution.py:31
  250.1 6.0 %collective-permute-done.12 = bf16[40,4096]{1,0:T(8,128)(2,1)} collective-permute-done((bf16[40,4096]{1,0:T(8,128)(2,1)}, bf16[40,4096]{1,0:T(8,128)(2,1)}, u32[]{:S(2)}, u32[]{:S(2)}) %collective-permute-start.12) | collective-permute-done | bytes 327712 | tf_op jit(solution)/shard_map/ppermute | solution.py:31
  256.2 18.1 %collective-permute-done.11 = bf16[40,4096]{1,0:T(8,128)(2,1)} collective-permute-done((bf16[40,4096]{1,0:T(8,128)(2,1)S(1)}, bf16[40,4096]{1,0:T(8,128)(2,1)}, u32[]{:S(2)}, u32[]{:S(2)}) %collective-permute-start.11) | collective-permute-done | bytes 327712 | tf_op jit(solution)/shard_map/ppermute | solution.py:31
  274.3 1.6 collective-permute-start.5
  275.9 2.0 collective-permute-start.3
  278.0 2.0 fusion.63
  280.0 1.3 collective-permute-start.23
  281.4 11.4 %collective-permute-start.22 = (bf16[24,4096]{1,0:T(8,128)(2,1)}, bf16[24,4096]{1,0:T(8,128)(2,1)S(1)}, u32[]{:S(2)}, u32[]{:S(2)}) collective-permute-start(bf16[24,4096]{1,0:T(8,128)(2,1)} %get-tuple-element.25), channel_id=1, source_target_pairs={{0,10},{2,12},{4,14},{6,0},{8,2},{10,4},{12,6},{14,8},{1,11},{3,13... | collective-permute-start | bytes 589832 | tf_op jit(solution)/shard_map/ppermute | solution.py:31
  292.8 18.0 %collective-permute-done.5 = bf16[64,4096]{1,0:T(8,128)(2,1)S(1)} collective-permute-done((bf16[64,4096]{1,0:T(8,128)(2,1)}, bf16[64,4096]{1,0:T(8,128)(2,1)S(1)}, u32[]{:S(2)}, u32[]{:S(2)}) %collective-permute-start.5) | collective-permute-done | bytes 524320 | tf_op jit(solution)/shard_map/ppermute | solution.py:31
  310.8 1.7 collective-permute-start.21
  312.5 8.9 %collective-permute-done.3 = bf16[64,4096]{1,0:T(8,128)(2,1)S(1)} collective-permute-done((bf16[64,4096]{1,0:T(8,128)(2,1)}, bf16[64,4096]{1,0:T(8,128)(2,1)S(1)}, u32[]{:S(2)}, u32[]{:S(2)}) %collective-permute-start.3) | collective-permute-done | bytes 524320 | tf_op jit(solution)/shard_map/ppermute | solution.py:31
  321.4 0.8 collective-permute-start.19
  322.2 2.1 fusion.44
  324.3 2.4 collective-permute-start.27
  326.7 1.6 collective-permute-start.17
  328.3 1.6 collective-permute-start.9
  329.9 1.3 fusion.74
  331.2 1.6 collective-permute-start.25
  332.8 0.5 maximum_bitcast_fusion.5
  333.3 18.2 %collective-permute-done.25 = bf16[24,4096]{1,0:T(8,128)(2,1)S(1)} collective-permute-done((bf16[24,4096]{1,0:T(8,128)(2,1)S(1)}, bf16[24,4096]{1,0:T(8,128)(2,1)S(1)}, u32[]{:S(2)}, u32[]{:S(2)}) %collective-permute-start.25) | collective-permute-done | bytes 196640 | tf_op jit(solution)/shard_map/ppermute | solution.py:21
  351.5 1.0 maximum_bitcast_fusion.4
  (66 shorter events, 1.4 us)
Async XLA Ops:
  7.2 98.0 %all-gather.2.cloned.1.call-start = ((), (), s32[]{:S(2)}) async-start(), calls=%async_computation | async-start | bytes 17825792 | tf_op jit(solution)/shard_map/all_gather | solution.py:58
  11.3 6.1 %collective-permute-start = (bf16[4096,384]{1,0:T(8,128)(2,1)}, bf16[4096,384]{1,0:T(8,128)(2,1)}, u32[]{:S(2)}, u32[]{:S(2)}) collective-permute-start(bf16[4096,384]{1,0:T(8,128)(2,1)} %bitcast.249), channel_id=1, source_target_pairs={{0,1},{1,0},{2,3},{3,2},{4,5},{5,4},{6,7},{7,6},{8,9},{9,8},{10,11... | collective-permute-start | bytes 9437192 | tf_op jit(solution)/shard_map/ppermute | solution.py:37
  11.4 135.0 %collective-permute-start.1 = (bf16[384,4096]{1,0:T(8,128)(2,1)}, bf16[384,4096]{1,0:T(8,128)(2,1)}, u32[]{:S(2)}, u32[]{:S(2)}) collective-permute-start(bf16[384,4096]{1,0:T(8,128)(2,1)} %bitcast.251), channel_id=1, source_target_pairs={{0,1},{1,0},{2,3},{3,2},{4,5},{5,4},{6,7},{7,6},{8,9},{9,8},{10,11... | collective-permute-start | bytes 9437192 | tf_op jit(solution)/shard_map/ppermute | solution.py:37
  138.5 23.4 %copy-start.4 = (bf16[2048,256]{0,1:T(8,128)(2,1)}, bf16[2048,256]{0,1:T(8,128)(2,1)S(1)}, u32[]{:S(2)}) copy-start(bf16[2048,256]{0,1:T(8,128)(2,1)S(1)} %convolution_convert_fusion.3) | copy-start | bytes 3145732
  144.0 2.5 copy-start.10
  149.8 3.2 copy-start.5
  151.0 60.8 %collective-permute-start.18 = (bf16[24,4096]{1,0:T(8,128)(2,1)}, bf16[24,4096]{1,0:T(8,128)(2,1)}, u32[]{:S(2)}, u32[]{:S(2)}) collective-permute-start(bf16[24,4096]{1,0:T(8,128)(2,1)} %get-tuple-element.22), channel_id=1, source_target_pairs={{0,2},{2,4},{4,6},{6,8},{8,10},{10,12},{12,14},{14,0},{1,3},{3,5},... | collective-permute-start | bytes 589832 | tf_op jit(solution)/shard_map/ppermute | solution.py:31
  152.6 62.7 %collective-permute-start.24 = (bf16[24,4096]{1,0:T(8,128)(2,1)}, bf16[24,4096]{1,0:T(8,128)(2,1)}, u32[]{:S(2)}, u32[]{:S(2)}) collective-permute-start(bf16[24,4096]{1,0:T(8,128)(2,1)} %get-tuple-element.23), channel_id=1, source_target_pairs={{0,14},{2,0},{4,2},{6,4},{8,6},{10,8},{12,10},{14,12},{1,15},{3,1}... | collective-permute-start | bytes 589832 | tf_op jit(solution)/shard_map/ppermute | solution.py:31
  171.4 4.2 %copy-start.3 = (bf16[320,4096]{1,0:T(8,128)(2,1)}, bf16[320,4096]{1,0:T(8,128)(2,1)S(1)}, u32[]{:S(2)}) copy-start(bf16[320,4096]{1,0:T(8,128)(2,1)S(1)} %convolution_convert_fusion.1) | copy-start | bytes 7864324
  172.8 43.8 %collective-permute-start.10 = (bf16[40,4096]{1,0:T(8,128)(2,1)}, bf16[40,4096]{1,0:T(8,128)(2,1)}, u32[]{:S(2)}, u32[]{:S(2)}) collective-permute-start(bf16[40,4096]{1,0:T(8,128)(2,1)} %get-tuple-element.15), channel_id=1, source_target_pairs={{0,2},{2,4},{4,6},{6,8},{8,10},{10,12},{12,14},{14,0},{1,3},{3,5},... | collective-permute-start | bytes 983048 | tf_op jit(solution)/shard_map/ppermute | solution.py:31
  175.3 42.3 %collective-permute-start.16 = (bf16[40,4096]{1,0:T(8,128)(2,1)}, bf16[40,4096]{1,0:T(8,128)(2,1)}, u32[]{:S(2)}, u32[]{:S(2)}) collective-permute-start(bf16[40,4096]{1,0:T(8,128)(2,1)} %get-tuple-element.16), channel_id=1, source_target_pairs={{0,14},{2,0},{4,2},{6,4},{8,6},{10,8},{12,10},{14,12},{1,15},{3,1}... | collective-permute-start | bytes 983048 | tf_op jit(solution)/shard_map/ppermute | solution.py:31
  182.4 8.9 %copy-start = (f32[2048,512,6]{1,0,2:T(8,128)}, f32[2048,512,6]{1,0,2:T(8,128)S(1)}, u32[]{:S(2)}) copy-start(f32[2048,512,6]{1,0,2:T(8,128)S(1)} %get-tuple-element.34) | copy-start | bytes 75497472
  191.4 12.1 %copy-start.11 = (bf16[1,384,4096]{2,1,0:T(8,128)(2,1)S(1)}, bf16[1,384,4096]{2,1,0:T(8,128)(2,1)}, u32[]{:S(2)}) copy-start(bf16[1,384,4096]{2,1,0:T(8,128)(2,1)} %param.9) | copy-start | bytes 9437188
  203.4 5.6 %collective-permute-start.26 = (f32[3]{0:T(128)S(1)}, f32[3]{0:T(128)S(1)}, u32[]{:S(2)}, u32[]{:S(2)}) collective-permute-start(f32[3]{0:T(128)S(1)} %slice.51), channel_id=1, source_target_pairs={{0,1},{1,0},{2,3},{3,2},{4,5},{5,4},{6,7},{7,6},{8,9},{9,8},{10,11... | collective-permute-start | bytes 44 | tf_op jit(solution)/shard_map/ppermute | solution.py:37
  203.5 5.5 %copy-start.7 = (bf16[40,4096]{1,0:T(8,128)(2,1)S(1)}, bf16[40,4096]{1,0:T(8,128)(2,1)}, u32[]{:S(2)}) copy-start(bf16[40,4096]{1,0:T(8,128)(2,1)} %get-tuple-element.17) | copy-start | bytes 983044
  203.5 8.3 %copy-start.6 = (bf16[40,4096]{1,0:T(8,128)(2,1)S(1)}, bf16[40,4096]{1,0:T(8,128)(2,1)}, u32[]{:S(2)}) copy-start(bf16[40,4096]{1,0:T(8,128)(2,1)} %get-tuple-element.18) | copy-start | bytes 983044
  209.0 4.6 %copy-start.2 = (bf16[512,4096]{1,0:T(8,128)(2,1)}, bf16[512,4096]{1,0:T(8,128)(2,1)S(1)}, u32[]{:S(2)}) copy-start(bf16[512,4096]{1,0:T(8,128)(2,1)S(1)} %convolution_convert_fusion) | copy-start | bytes 12582916
  209.0 37.2 %copy-start.1 = (bf16[1,1,128,4096]{3,2,1,0:T(8,128)(2,1)S(1)}, bf16[1,1,128,4096]{3,2,1,0:T(8,128)(2,1)}, u32[]{:S(2)}) copy-start(bf16[1,1,128,4096]{3,2,1,0:T(8,128)(2,1)} %param.5) | copy-start | bytes 3145732
  209.0 35.7 %collective-permute-start.15 = (bf16[40,4096]{1,0:T(8,128)(2,1)S(1)}, bf16[40,4096]{1,0:T(8,128)(2,1)S(1)}, u32[]{:S(2)}, u32[]{:S(2)}) collective-permute-start(bf16[40,4096]{1,0:T(8,128)(2,1)S(1)} %copy-done.7), channel_id=1, source_target_pairs={{0,12},{2,14},{4,0},{6,2},{8,4},{10,6},{12,8},{14,10},{1,13},{3,15... | collective-permute-start | bytes 983048 | tf_op jit(solution)/shard_map/ppermute | solution.py:31
  211.8 32.9 %collective-permute-start.14 = (bf16[40,4096]{1,0:T(8,128)(2,1)S(1)}, bf16[40,4096]{1,0:T(8,128)(2,1)S(1)}, u32[]{:S(2)}, u32[]{:S(2)}) collective-permute-start(bf16[40,4096]{1,0:T(8,128)(2,1)S(1)} %copy-done.6), channel_id=1, source_target_pairs={{0,10},{2,12},{4,14},{6,0},{8,2},{10,4},{12,6},{14,8},{1,11},{3,13... | collective-permute-start | bytes 983048 | tf_op jit(solution)/shard_map/ppermute | solution.py:31
  215.4 60.5 %collective-permute-start.2 = (bf16[64,4096]{1,0:T(8,128)(2,1)}, bf16[64,4096]{1,0:T(8,128)(2,1)}, u32[]{:S(2)}, u32[]{:S(2)}) collective-permute-start(bf16[64,4096]{1,0:T(8,128)(2,1)} %get-tuple-element.8), channel_id=1, source_target_pairs={{0,2},{2,4},{4,6},{6,8},{8,10},{10,12},{12,14},{14,0},{1,3},{3,5},... | collective-permute-start | bytes 1572872 | tf_op jit(solution)/shard_map/ppermute | solution.py:31
  216.6 59.4 %collective-permute-start.8 = (bf16[64,4096]{1,0:T(8,128)(2,1)}, bf16[64,4096]{1,0:T(8,128)(2,1)}, u32[]{:S(2)}, u32[]{:S(2)}) collective-permute-start(bf16[64,4096]{1,0:T(8,128)(2,1)} %get-tuple-element.9), channel_id=1, source_target_pairs={{0,14},{2,0},{4,2},{6,4},{8,6},{10,8},{12,10},{14,12},{1,15},{3,1}... | collective-permute-start | bytes 1572872 | tf_op jit(solution)/shard_map/ppermute | solution.py:31
  217.6 28.8 %collective-permute-start.13 = (bf16[40,4096]{1,0:T(8,128)(2,1)}, bf16[40,4096]{1,0:T(8,128)(2,1)}, u32[]{:S(2)}, u32[]{:S(2)}) collective-permute-start(bf16[40,4096]{1,0:T(8,128)(2,1)} %get-tuple-element.19), channel_id=1, source_target_pairs={{0,8},{2,10},{4,12},{6,14},{8,0},{10,2},{12,4},{14,6},{1,9},{3,11}... | collective-permute-start | bytes 983048 | tf_op jit(solution)/shard_map/ppermute | solution.py:31
  244.7 0.7 copy-start.8
  244.7 11.5 %collective-permute-start.12 = (bf16[40,4096]{1,0:T(8,128)(2,1)}, bf16[40,4096]{1,0:T(8,128)(2,1)}, u32[]{:S(2)}, u32[]{:S(2)}) collective-permute-start(bf16[40,4096]{1,0:T(8,128)(2,1)} %get-tuple-element.20), channel_id=1, source_target_pairs={{0,6},{2,8},{4,10},{6,12},{8,14},{10,0},{12,2},{14,4},{1,7},{3,9},... | collective-permute-start | bytes 983048 | tf_op jit(solution)/shard_map/ppermute | solution.py:31
  245.4 0.7 copy-start.9
  246.2 28.2 %collective-permute-start.11 = (bf16[40,4096]{1,0:T(8,128)(2,1)S(1)}, bf16[40,4096]{1,0:T(8,128)(2,1)}, u32[]{:S(2)}, u32[]{:S(2)}) collective-permute-start(bf16[40,4096]{1,0:T(8,128)(2,1)S(1)} %get-tuple-element.21), channel_id=1, source_target_pairs={{0,4},{2,6},{4,8},{6,10},{8,12},{10,14},{12,0},{14,2},{1,5},{3,7},... | collective-permute-start | bytes 983048 | tf_op jit(solution)/shard_map/ppermute | solution.py:31
  246.4 33.6 %collective-permute-start.7 = (bf16[64,4096]{1,0:T(8,128)(2,1)}, bf16[64,4096]{1,0:T(8,128)(2,1)S(1)}, u32[]{:S(2)}, u32[]{:S(2)}) collective-permute-start(bf16[64,4096]{1,0:T(8,128)(2,1)} %get-tuple-element.10), channel_id=1, source_target_pairs={{0,12},{2,14},{4,0},{6,2},{8,4},{10,6},{12,8},{14,10},{1,13},{3,15... | collective-permute-start | bytes 1572872 | tf_op jit(solution)/shard_map/ppermute | solution.py:31
  256.2 25.2 %collective-permute-start.6 = (bf16[64,4096]{1,0:T(8,128)(2,1)}, bf16[64,4096]{1,0:T(8,128)(2,1)S(1)}, u32[]{:S(2)}, u32[]{:S(2)}) collective-permute-start(bf16[64,4096]{1,0:T(8,128)(2,1)} %get-tuple-element.11), channel_id=1, source_target_pairs={{0,10},{2,12},{4,14},{6,0},{8,2},{10,4},{12,6},{14,8},{1,11},{3,13... | collective-permute-start | bytes 1572872 | tf_op jit(solution)/shard_map/ppermute | solution.py:31
  274.3 36.5 %collective-permute-start.5 = (bf16[64,4096]{1,0:T(8,128)(2,1)}, bf16[64,4096]{1,0:T(8,128)(2,1)S(1)}, u32[]{:S(2)}, u32[]{:S(2)}) collective-permute-start(bf16[64,4096]{1,0:T(8,128)(2,1)} %get-tuple-element.12), channel_id=1, source_target_pairs={{0,8},{2,10},{4,12},{6,14},{8,0},{10,2},{12,4},{14,6},{1,9},{3,11}... | collective-permute-start | bytes 1572872 | tf_op jit(solution)/shard_map/ppermute | solution.py:31
  275.9 36.5 %collective-permute-start.4 = (bf16[64,4096]{1,0:T(8,128)(2,1)}, bf16[64,4096]{1,0:T(8,128)(2,1)S(1)}, u32[]{:S(2)}, u32[]{:S(2)}) collective-permute-start(bf16[64,4096]{1,0:T(8,128)(2,1)} %get-tuple-element.13), channel_id=1, source_target_pairs={{0,6},{2,8},{4,10},{6,12},{8,14},{10,0},{12,2},{14,4},{1,7},{3,9},... | collective-permute-start | bytes 1572872 | tf_op jit(solution)/shard_map/ppermute | solution.py:31
  275.9 45.5 %collective-permute-start.3 = (bf16[64,4096]{1,0:T(8,128)(2,1)}, bf16[64,4096]{1,0:T(8,128)(2,1)S(1)}, u32[]{:S(2)}, u32[]{:S(2)}) collective-permute-start(bf16[64,4096]{1,0:T(8,128)(2,1)} %get-tuple-element.14), channel_id=1, source_target_pairs={{0,4},{2,6},{4,8},{6,10},{8,12},{10,14},{12,0},{14,2},{1,5},{3,7},... | collective-permute-start | bytes 1572872 | tf_op jit(solution)/shard_map/ppermute | solution.py:31
  280.0 44.2 %collective-permute-start.23 = (bf16[24,4096]{1,0:T(8,128)(2,1)}, bf16[24,4096]{1,0:T(8,128)(2,1)S(1)}, u32[]{:S(2)}, u32[]{:S(2)}) collective-permute-start(bf16[24,4096]{1,0:T(8,128)(2,1)} %get-tuple-element.24), channel_id=1, source_target_pairs={{0,12},{2,14},{4,0},{6,2},{8,4},{10,6},{12,8},{14,10},{1,13},{3,15... | collective-permute-start | bytes 589832 | tf_op jit(solution)/shard_map/ppermute | solution.py:31
  281.4 45.4 %collective-permute-start.22 = (bf16[24,4096]{1,0:T(8,128)(2,1)}, bf16[24,4096]{1,0:T(8,128)(2,1)S(1)}, u32[]{:S(2)}, u32[]{:S(2)}) collective-permute-start(bf16[24,4096]{1,0:T(8,128)(2,1)} %get-tuple-element.25), channel_id=1, source_target_pairs={{0,10},{2,12},{4,14},{6,0},{8,2},{10,4},{12,6},{14,8},{1,11},{3,13... | collective-permute-start | bytes 589832 | tf_op jit(solution)/shard_map/ppermute | solution.py:31
  310.8 17.5 %collective-permute-start.21 = (bf16[24,4096]{1,0:T(8,128)(2,1)}, bf16[24,4096]{1,0:T(8,128)(2,1)S(1)}, u32[]{:S(2)}, u32[]{:S(2)}) collective-permute-start(bf16[24,4096]{1,0:T(8,128)(2,1)} %get-tuple-element.26), channel_id=1, source_target_pairs={{0,8},{2,10},{4,12},{6,14},{8,0},{10,2},{12,4},{14,6},{1,9},{3,11}... | collective-permute-start | bytes 589832 | tf_op jit(solution)/shard_map/ppermute | solution.py:31
  312.5 17.4 %collective-permute-start.20 = (bf16[24,4096]{1,0:T(8,128)(2,1)}, bf16[24,4096]{1,0:T(8,128)(2,1)S(1)}, u32[]{:S(2)}, u32[]{:S(2)}) collective-permute-start(bf16[24,4096]{1,0:T(8,128)(2,1)} %get-tuple-element.27), channel_id=1, source_target_pairs={{0,6},{2,8},{4,10},{6,12},{8,14},{10,0},{12,2},{14,4},{1,7},{3,9},... | collective-permute-start | bytes 589832 | tf_op jit(solution)/shard_map/ppermute | solution.py:31
  321.4 8.4 %collective-permute-start.19 = (bf16[24,4096]{1,0:T(8,128)(2,1)}, bf16[24,4096]{1,0:T(8,128)(2,1)S(1)}, u32[]{:S(2)}, u32[]{:S(2)}) collective-permute-start(bf16[24,4096]{1,0:T(8,128)(2,1)} %get-tuple-element.28), channel_id=1, source_target_pairs={{0,4},{2,6},{4,8},{6,10},{8,12},{10,14},{12,0},{14,2},{1,5},{3,7},... | collective-permute-start | bytes 589832 | tf_op jit(solution)/shard_map/ppermute | solution.py:31
  324.3 8.5 %collective-permute-start.27 = (f32[3]{0:T(128)S(1)}, f32[3]{0:T(128)S(1)}, u32[]{:S(2)}, u32[]{:S(2)}) collective-permute-start(f32[3]{0:T(128)S(1)} %slice_maximum_fusion), channel_id=1, source_target_pairs={{64,0},{0,64},{65,1},{1,65},{66,2},{2,66},{67,3},{3,67},{68,4},{4,... | collective-permute-start | bytes 44 | tf_op jit(solution)/shard_map/ppermute | solution.py:21
  326.7 24.8 %collective-permute-start.17 = (bf16[40,4096]{1,0:T(8,128)(2,1)S(1)}, bf16[40,4096]{1,0:T(8,128)(2,1)S(1)}, u32[]{:S(2)}, u32[]{:S(2)}) collective-permute-start(bf16[40,4096]{1,0:T(8,128)(2,1)S(1)} %fusion.63), channel_id=1, source_target_pairs={{48,0},{0,16},{16,32},{32,48},{49,1},{1,17},{17,33},{33,49},{50,2}... | collective-permute-start | bytes 983048 | tf_op jit(solution)/shard_map/ppermute | solution.py:21
  328.3 23.3 %collective-permute-start.9 = (bf16[64,4096]{1,0:T(8,128)(2,1)S(1)}, bf16[64,4096]{1,0:T(8,128)(2,1)S(1)}, u32[]{:S(2)}, u32[]{:S(2)}) collective-permute-start(bf16[64,4096]{1,0:T(8,128)(2,1)S(1)} %fusion.44), channel_id=1, source_target_pairs={{48,0},{0,16},{16,32},{32,48},{49,1},{1,17},{17,33},{33,49},{50,2}... | collective-permute-start | bytes 1572872 | tf_op jit(solution)/shard_map/ppermute | solution.py:21
  331.2 20.3 %collective-permute-start.25 = (bf16[24,4096]{1,0:T(8,128)(2,1)S(1)}, bf16[24,4096]{1,0:T(8,128)(2,1)S(1)}, u32[]{:S(2)}, u32[]{:S(2)}) collective-permute-start(bf16[24,4096]{1,0:T(8,128)(2,1)S(1)} %fusion.74), channel_id=1, source_target_pairs={{48,0},{0,16},{16,32},{32,48},{49,1},{1,17},{17,33},{33,49},{50,2}... | collective-permute-start | bytes 589832 | tf_op jit(solution)/shard_map/ppermute | solution.py:21
Sparse Core Ops, SparseCore 0:
  11.4 93.7 all-gather.1
